TPU v7x, 128 devices: a whole 4x4x4 slice. The times are simulated.
128 devices in a mesh: wl: 8 (over x, z_hi), tile: 16 (over z_lo, y, core).
Axes of the slice: x: 4, y: 4, z: 4 (z_hi: 2, z_lo: 2; z = z_hi * 2 + z_lo), core: 2. Of those that a mesh axis runs over, the one named last changes fastest.
Arguments:
- density: float32 [32, 1024], P('tile', 'wl'), may hold values from 0 to 1
- foot_index: int32 [4, 128, 4096], P(None, 'tile'), may hold values from 0 to 2047, as said below
- foot_weight: bfloat16 [4, 128, 4096], P(None, 'tile'), may hold values from 0.099609375 to 0.3984375
- source_fwd: float32 [16, 128, 4096], P('wl', 'tile'), may hold values from -6 to 6
- source_adj: float32 [16, 128, 4096], P('wl', 'tile'), may hold values from -6 to 6
- omega: float32 [16], P('wl'), may hold values from 0.2 to 1.5
Outputs:
- forward_field: float32 [16, 128, 4096], P('wl', 'tile')
- density_grad: float32 [32, 1024], P('tile', 'wl')
Inputs may be any that keep to these rules, and one draw needn't show every extreme that they name: foot_index[f, x, y] = r * 1024 + c names coarse row r and column c of the strip of the tile holding row x, with r within one of (x mod 8) // 4 and c within two of y // 4; entry f = 0 is the cell's own block.
All inputs are finite; a program needn't handle non-finite values.
Results may differ from a plain program's by a relative error of at most 0.0003.
Values sent between devices are 32-bit elements; how exact they have to be, the bound alone decides.
No kernel may reach another device: no remote copies, remote signals or barrier semaphores. Data moves between devices by JAX's collectives and lax.ppermute only.
A program may use at most 192 MiB of HBM per device.

v0:
```python
import jax
import jax.numpy as jnp
from jax import lax
from jax.sharding import PartitionSpec as P

ITERS = 4
HALO = 4
SHIFTS = (-2, -1, 0, 1, 2)
time_step = 0.5
high_contrast = 4.0
drude_decay = 0.9
drude_gain = 0.5


def from_behind(value, axis, steps):
    count = lax.axis_size(axis)
    first, last = (max(0, -steps), min(count, count - steps))
    return lax.ppermute(value, axis, [(source, source + steps) for source in range(first, last)])


def with_halo(value, axis):
    above = from_behind(value[..., -HALO:, :], axis, 1)
    below = from_behind(value[..., :HALO, :], axis, -1)
    return jnp.concatenate([above, value, below], axis=-2)


def lane_shift(vector, shift):
    width = vector.shape[-1]
    pad = [(0, 0)] * (vector.ndim - 1) + [(abs(shift), abs(shift))]
    padded = jnp.pad(vector, pad)
    start = abs(shift) - shift
    return lax.slice_in_dim(padded, start, start + width, axis=vector.ndim - 1)


def march(source, drive, density_cell, inverse, valid):
    field_e = jnp.zeros_like(source)
    field_hx = jnp.zeros_like(source)
    field_hy = jnp.zeros_like(source)
    current = jnp.zeros_like(source)
    rows = source.shape[2]
    history = []
    for turn in range(ITERS):
        row_zero = jnp.zeros_like(source[:, :, :1, :])
        col_zero = jnp.zeros_like(source[:, :, :, :1])
        e_up = jnp.concatenate([field_e[:, :, 1:, :], row_zero], 2)
        e_right = jnp.concatenate([field_e[:, :, :, 1:], col_zero], 3)
        field_hx = field_hx - time_step * (e_right - field_e)
        field_hy = (field_hy + time_step * (e_up - field_e)) * valid
        current = drude_decay * current + drude_gain * density_cell * field_e
        hy_down = jnp.concatenate([row_zero, field_hy[:, :, :-1, :]], 2)
        hx_left = jnp.concatenate([col_zero, field_hx[:, :, :, :-1]], 3)
        field_e = (
            field_e
            + inverse * (field_hy - hy_down - (field_hx - hx_left) - current)
            + drive[turn] * source
        ) * valid
        history.append(field_e[:, :, HALO : rows - HALO, :])
    return history


def shards(density, foot_index, foot_weight, source_fwd, source_adj, omega):
    sources = jnp.stack([source_fwd, source_adj])
    sources_ext = with_halo(sources, "tile")
    strip = lax.all_gather(density, "wl", axis=1, tiled=True)
    block_rows, block_cols = strip.shape
    cells_x, cells_y = foot_index.shape[1:]
    factor = cells_y // block_cols
    weights = foot_weight.astype(jnp.float32)
    col_block = lax.broadcasted_iota(jnp.int32, (1, cells_y), 1) // factor
    key = foot_index // block_cols * len(SHIFTS) + (foot_index % block_cols - col_block[None]) + 2
    upsampled = jnp.repeat(strip, factor, axis=1)
    matched = []
    density_cell = jnp.zeros((cells_x, cells_y), jnp.float32)
    for row in range(block_rows):
        for slot, shift in enumerate(SHIFTS):
            code = row * len(SHIFTS) + slot
            weight_sum = jnp.sum(jnp.where(key == code, weights, 0.0), axis=0)
            matched.append(weight_sum)
            density_cell = (
                density_cell + weight_sum * lane_shift(upsampled[row], -factor * shift)[None]
            )
    density_ext = with_halo(density_cell, "tile")
    inverse_ext = time_step / (1.0 + high_contrast * density_ext)
    rows_ext = cells_x + 2 * HALO
    global_row = (
        lax.axis_index("tile") * cells_x - HALO + lax.broadcasted_iota(jnp.int32, (rows_ext, 1), 0)
    )
    valid = ((global_row >= 0) & (global_row < cells_x * lax.axis_size("tile"))).astype(jnp.float32)
    drive = [jnp.sin(omega * (turn + 1.0))[None, :, None, None] for turn in range(ITERS)]
    history = march(sources_ext, drive, density_ext, inverse_ext, valid)
    sense = jnp.zeros((cells_x, cells_y), jnp.float32)
    for turn in range(ITERS):
        sense = sense + jnp.sum(history[turn][1] * history[ITERS - 1 - turn][0], axis=0)
    total_waves = source_fwd.shape[0] * lax.axis_size("wl")
    scaled = high_contrast / total_waves * sense
    pooled_rows = []
    for row in range(block_rows):
        acc = jnp.zeros((cells_y,), jnp.float32)
        for slot, shift in enumerate(SHIFTS):
            per_col = jnp.sum(matched[row * len(SHIFTS) + slot] * scaled, axis=0)
            acc = acc + lane_shift(per_col, factor * shift)
        pooled_rows.append(acc.reshape(block_cols, factor).sum(axis=1))
    partial_grad = jnp.stack(pooled_rows)
    density_grad = lax.psum_scatter(partial_grad, "wl", scatter_dimension=1, tiled=True)
    return (history[ITERS - 1][0], density_grad)


def solution(mesh):
    in_specs = (
        P("tile", "wl"),
        P(None, "tile", None),
        P(None, "tile", None),
        P("wl", "tile", None),
        P("wl", "tile", None),
        P("wl"),
    )
    out_specs = (P("wl", "tile", None), P("tile", "wl"))
    return jax.shard_map(shards, mesh=mesh, in_specs=in_specs, out_specs=out_specs, check_vma=False)
```

profile of v0, /device:TPU:0, one launch (start us, length us, event | category | flops | bytes accessed | tf_op | source)
XLA Modules:
  0.0 138.3 jit_solution(15025737107666634582)
XLA Ops:
  7.2 0.6 copy-done.4
  7.8 24.2 %all_gather.3 = f32[2,1024]{1,0:T(2,128)S(1)} all-gather(f32[2,128]{1,0:T(2,128)S(1)} %copy-done.4), channel_id=1, replica_groups=mesh['wl'=8,'tile'=16] {'wl'}, dimensions={1}, use_global_device_ids=true | all-gather | bytes 9216 | tf_op jit(solution)/shard_map/all_gather | solution.py:64
  32.1 0.2 broadcast_in_dim.24
  32.3 0.3 broadcast_in_dim.25
  32.6 0.2 broadcast_in_dim.22
  32.8 0.3 broadcast_in_dim.23
  33.1 0.1 pad_slice_fusion.5
  33.2 0.5 copy-done.2
  33.6 0.2 copy-done.3
  33.8 1.1 fusion.4
  34.8 0.1 multiply_add_fusion.2
  35.0 1.4 %collective-permute-start.1 = (f32[4,4096]{1,0:T(4,128)S(1)}, f32[4,4096]{1,0:T(4,128)S(1)}, u32[]{:S(2)}, u32[]{:S(2)}) collective-permute-start(f32[4,4096]{1,0:T(4,128)S(1)} %get-tuple-element.38), channel_id=1, source_target_pairs={{1,0},{2,1},{3,2},{4,3},{5,4},{6,5},{7,6},{8,7},{9,8},{10,9},{11,1... | collective-permute-start | bytes 196616 | tf_op jit(solution)/shard_map/ppermute | solution.py:18
  36.5 3.0 %collective-permute-start = (f32[4,4096]{1,0:T(4,128)S(1)}, f32[4,4096]{1,0:T(4,128)S(1)}, u32[]{:S(2)}, u32[]{:S(2)}) collective-permute-start(f32[4,4096]{1,0:T(4,128)S(1)} %get-tuple-element.37), channel_id=1, source_target_pairs={{0,1},{1,2},{2,3},{3,4},{4,5},{5,6},{6,7},{7,8},{8,9},{9,10},{10,1... | collective-permute-start | bytes 196616 | tf_op jit(solution)/shard_map/ppermute | solution.py:18
  39.5 0.1 fusion.18
  39.6 1.3 collective-permute-start.3
  40.9 3.7 %collective-permute-start.2 = (f32[2,2,4,4096]{3,2,1,0:T(4,128)S(1)}, f32[2,2,4,4096]{3,2,1,0:T(4,128)S(1)}, u32[]{:S(2)}, u32[]{:S(2)}) collective-permute-start(f32[2,2,4,4096]{3,2,1,0:T(4,128)S(1)} %get-tuple-element.32), channel_id=1, source_target_pairs={{0,1},{1,2},{2,3},{3,4},{4,5},{5,6},{6,7},{7,8},{8,9},{9,10},{10,1... | collective-permute-start | bytes 786440 | tf_op jit(solution)/shard_map/ppermute | solution.py:18
  44.7 0.6 copy-done.5
  45.3 0.1 multiply_sine_fusion
  45.4 0.1 pad_subtract_fusion
  45.5 0.1 pad_subtract_fusion.1
  45.6 0.1 broadcast_multiply_fusion.1
  45.7 0.1 collective-permute-done.2
  45.8 0.3 add_multiply_fusion.6
  46.1 0.1 slice.288
  46.2 0.3 slice.290
  46.5 0.6 add_multiply_fusion.5
  47.1 0.9 add_multiply_fusion.4
  48.0 0.1 slice.292
  48.1 0.3 slice.294
  48.4 0.4 add_multiply_fusion.3
  48.9 1.0 add_multiply_fusion.2
  49.9 0.1 slice.296
  50.0 0.3 slice.298
  50.3 0.4 add_multiply_fusion.1
  50.7 1.1 add_multiply_fusion
  51.9 0.8 fusion.23
  52.6 0.1 fusion.19
  52.7 0.1 fusion.21
  52.8 0.4 multiply_reduce_fusion.5
  53.2 0.1 fusion.31
  53.3 0.5 add.288
  53.9 0.2 reduce_sum.259
  54.1 0.1 fusion.27
  54.2 0.5 add.283
  54.7 0.2 reduce_sum.253
  54.9 1.0 copy.8
  56.0 74.0 %reduce-scatter.4.cloned.1.call-done = f32[128,2]{1,0:T(8,128)} async-done(((f32[1024,2]{1,0:T(8,128)}), f32[128,2]{1,0:T(8,128)}) %reduce-scatter.4.cloned.1.call-update) | async-done | bytes 1040
  130.0 1.5 %copy.9 = f32[2,128]{1,0:T(2,128)} copy(f32[2,128]{0,1:T(8,128)} %bitcast.45) | data formatting | bytes 2048
  (22 shorter events, 0.2 us)
Async XLA Ops:
  7.2 0.7 copy-start.4
  7.2 122.8 %reduce-scatter.4.cloned.1.call-start = ((), (), s32[]{:S(2)}) async-start(), calls=%async_computation.1 | async-start | bytes 589824
  32.6 1.0 copy-start.2
  32.8 1.0 copy-start.3
  34.8 4.7 %copy-start.1 = (f32[2,8,4096]{2,1,0:T(8,128)S(1)}, f32[2,8,4096]{2,1,0:T(8,128)}, u32[]{:S(2)}) copy-start(f32[2,8,4096]{2,1,0:T(8,128)} %param.10) | copy-start | bytes 786436
  35.0 4.5 %copy-start = (f32[2,8,4096]{2,1,0:T(8,128)S(1)}, f32[2,8,4096]{2,1,0:T(8,128)}, u32[]{:S(2)}) copy-start(f32[2,8,4096]{2,1,0:T(8,128)} %param.9) | copy-start | bytes 786436
  35.0 10.6 %collective-permute-start.1 = (f32[4,4096]{1,0:T(4,128)S(1)}, f32[4,4096]{1,0:T(4,128)S(1)}, u32[]{:S(2)}, u32[]{:S(2)}) collective-permute-start(f32[4,4096]{1,0:T(4,128)S(1)} %get-tuple-element.38), channel_id=1, source_target_pairs={{1,0},{2,1},{3,2},{4,3},{5,4},{6,5},{7,6},{8,7},{9,8},{10,9},{11,1... | collective-permute-start | bytes 196616 | tf_op jit(solution)/shard_map/ppermute | solution.py:18
  36.5 9.1 %collective-permute-start = (f32[4,4096]{1,0:T(4,128)S(1)}, f32[4,4096]{1,0:T(4,128)S(1)}, u32[]{:S(2)}, u32[]{:S(2)}) collective-permute-start(f32[4,4096]{1,0:T(4,128)S(1)} %get-tuple-element.37), channel_id=1, source_target_pairs={{0,1},{1,2},{2,3},{3,4},{4,5},{5,6},{6,7},{7,8},{8,9},{9,10},{10,1... | collective-permute-start | bytes 196616 | tf_op jit(solution)/shard_map/ppermute | solution.py:18
  39.6 6.1 %collective-permute-start.3 = (f32[2,2,4,4096]{3,2,1,0:T(4,128)S(1)}, f32[2,2,4,4096]{3,2,1,0:T(4,128)S(1)}, u32[]{:S(2)}, u32[]{:S(2)}) collective-permute-start(f32[2,2,4,4096]{3,2,1,0:T(4,128)S(1)} %get-tuple-element.33), channel_id=1, source_target_pairs={{1,0},{2,1},{3,2},{4,3},{5,4},{6,5},{7,6},{8,7},{9,8},{10,9},{11,1... | collective-permute-start | bytes 786440 | tf_op jit(solution)/shard_map/ppermute | solution.py:18
  40.9 4.9 %collective-permute-start.2 = (f32[2,2,4,4096]{3,2,1,0:T(4,128)S(1)}, f32[2,2,4,4096]{3,2,1,0:T(4,128)S(1)}, u32[]{:S(2)}, u32[]{:S(2)}) collective-permute-start(f32[2,2,4,4096]{3,2,1,0:T(4,128)S(1)} %get-tuple-element.32), channel_id=1, source_target_pairs={{0,1},{1,2},{2,3},{3,4},{4,5},{5,6},{6,7},{7,8},{8,9},{9,10},{10,1... | collective-permute-start | bytes 786440 | tf_op jit(solution)/shard_map/ppermute | solution.py:18
  44.7 0.7 copy-start.5
Sparse Core Ops, SparseCore 0:
  56.1 73.8 reduce-scatter.3
where the time goes:
time: 139 us; the launch traced here: 138 us
  waiting for transfers between devices  74.1 us (53%)
  blocking collectives  24.2 us (17%)
  between operations  14.3 us (10%)
  starting transfers between devices  9.53 us (7%)
  other arithmetic  8.32 us (6%)
  local copies, waits for them, and re-layouts  7.76 us (6%)
    unnamed x2, waiting for transfers between devices  74 us
    all_gather x1, blocking collectives, shards(): strip = lax.all_gather(density, 'wl', axis=1, tiled=True)  24.2 us
    ppermute x4, starting transfers between devices, from_behind(): lax.ppermute(value, axis, [(source, source + steps) for source in range(f...  9.49 us
    unnamed x14, local copies, waits for them, and re-layouts  4.38 us
    mul x4, other arithmetic, march(): (field_e + inverse * (field_hy - hy_down - (field_hx - hx_left) - current...  3.26 us
  transfers between devices with their start and end apart: 5, of which 2 were waited for; matrix products, arithmetic and copies ran while one was open for 0% of the time, Pallas kernels for 0%

commit v1 on v0

--- a/solution.py
+++ b/solution.py
@@ -2,6 +2,7 @@
 import jax.numpy as jnp
 from jax import lax
 from jax.sharding import PartitionSpec as P
+from jax.lax import all_to_all, axis_size
 
 ITERS = 4
 HALO = 4
@@ -61,7 +62,7 @@
 def shards(density, foot_index, foot_weight, source_fwd, source_adj, omega):
     sources = jnp.stack([source_fwd, source_adj])
     sources_ext = with_halo(sources, "tile")
-    strip = lax.all_gather(density, "wl", axis=1, tiled=True)
+    strip = jnp.concatenate(all_to_all(jnp.stack([density] * axis_size("wl")), "wl", 0, 0), axis=1)
     block_rows, block_cols = strip.shape
     cells_x, cells_y = foot_index.shape[1:]
     factor = cells_y // block_cols

time: 139 us -> 129 us (0.928)
  blocking collectives: 24.2 us -> 0 us
  starting transfers between devices: 9.53 us -> 17.1 us
  waiting for transfers between devices: 74.1 us -> 79.6 us
    all_gather x1 -> x0, blocking collectives: 24.2 us -> none  [shards(): strip = lax.all_gather(density, 'wl', axis=1, tiled=True)]
    all_to_all x0 -> x1, starting transfers between devices: none -> 7.7 us  [shards(): all_to_all(jnp.stack([density] * axis_size('wl')), 'wl', 0, 0)]
    unnamed x2, waiting for transfers between devices: 74 us -> 78.8 us
    unnamed x14 -> x12, local copies, waits for them, and re-layouts: 4.38 us -> 3.25 us
  transfers between devices with their start and end apart: 5 -> 6, of which waited for: 2 -> 2; matrix products, arithmetic and copies ran while one was open for 0% -> 3% of each run, Pallas kernels for 0% -> 0%
where the time goes in v1:
time: 129 us
  waiting for transfers between devices  79.6 us (62%)
  starting transfers between devices  17.1 us (13%)
  between operations  14.3 us (11%)
  other arithmetic  9.62 us (7%)
  local copies, waits for them, and re-layouts  7.91 us (6%)
    unnamed x2, waiting for transfers between devices  78.8 us
    ppermute x4, starting transfers between devices, from_behind(): lax.ppermute(value, axis, [(source, source + steps) for source in range(f...  9.35 us
    all_to_all x1, starting transfers between devices, shards(): all_to_all(jnp.stack([density] * axis_size('wl')), 'wl', 0, 0)  7.7 us
    mul x4, other arithmetic, march(): (field_e + inverse * (field_hy - hy_down - (field_hx - hx_left) - current...  3.28 us
    unnamed x12, local copies, waits for them, and re-layouts  3.25 us
  transfers between devices with their start and end apart: 6, of which 2 were waited for; matrix products, arithmetic and copies ran while one was open for 3% of the time, Pallas kernels for 0%

profile of v1, /device:TPU:0, one launch (start us, length us, event | category | flops | bytes accessed | tf_op | source)
XLA Modules:
  0.0 128.5 jit_solution(17491638563863864280)
XLA Ops:
  7.2 1.3 stack.14
  8.4 7.7 %all-to-all-start = ((f32[8,2,128]{2,1,0:T(2,128)}), f32[8,2,128]{2,1,0:T(2,128)S(1)}, u32[]{:S(2)}, u32[]{:S(2)}) async-start(f32[8,2,128]{2,1,0:T(2,128)} %stack.14), calls=%async_computation | async-start | bytes 16384 | tf_op jit(solution)/shard_map/all_to_all | solution.py:65
  16.1 0.0 reduce-scatter.4.cloned.1.call-start
  16.2 1.4 %fusion.18 = (f32[2,2,4,4096]{3,2,1,0:T(4,128)S(1)}, f32[2,2,4,4096]{3,2,1,0:T(4,128)S(1)}) fusion(f32[1,2,8,4096]{3,2,1,0:T(8,128)} %bitcast.32, f32[1,2,8,4096]{3,2,1,0:T(8,128)} %bitcast.38), kind=kLoop, calls=%fused_computation.49 | loop fusion | flops 131072 | bytes 1048576 | tf_op jit(solution)/shard_map/stack | solution.py:63
  17.6 1.3 %collective-permute-start.3 = (f32[2,2,4,4096]{3,2,1,0:T(4,128)S(1)}, f32[2,2,4,4096]{3,2,1,0:T(4,128)S(1)}, u32[]{:S(2)}, u32[]{:S(2)}) collective-permute-start(f32[2,2,4,4096]{3,2,1,0:T(4,128)S(1)} %get-tuple-element.33), channel_id=1, source_target_pairs={{1,0},{2,1},{3,2},{4,3},{5,4},{6,5},{7,6},{8,7},{9,8},{10,9},{11,1... | collective-permute-start | bytes 786440 | tf_op jit(solution)/shard_map/ppermute | solution.py:19
  18.9 3.0 %collective-permute-start.2 = (f32[2,2,4,4096]{3,2,1,0:T(4,128)S(1)}, f32[2,2,4,4096]{3,2,1,0:T(4,128)S(1)}, u32[]{:S(2)}, u32[]{:S(2)}) collective-permute-start(f32[2,2,4,4096]{3,2,1,0:T(4,128)S(1)} %get-tuple-element.32), channel_id=1, source_target_pairs={{0,1},{1,2},{2,3},{3,4},{4,5},{5,6},{6,7},{7,8},{8,9},{9,10},{10,1... | collective-permute-start | bytes 786440 | tf_op jit(solution)/shard_map/ppermute | solution.py:19
  22.0 0.6 copy-done.4
  22.6 0.1 multiply_sine_fusion
  22.7 0.1 pad_subtract_fusion
  22.8 1.1 fusion.4
  23.9 0.2 broadcast_in_dim.24
  24.1 0.3 broadcast_in_dim.25
  24.4 0.2 broadcast_in_dim.22
  24.6 0.3 broadcast_in_dim.23
  24.8 0.1 pad_slice_fusion.5
  24.9 0.1 multiply_add_fusion.2
  25.1 1.3 %collective-permute-start.1 = (f32[4,4096]{1,0:T(4,128)S(1)}, f32[4,4096]{1,0:T(4,128)S(1)}, u32[]{:S(2)}, u32[]{:S(2)}) collective-permute-start(f32[4,4096]{1,0:T(4,128)S(1)} %get-tuple-element.38), channel_id=1, source_target_pairs={{1,0},{2,1},{3,2},{4,3},{5,4},{6,5},{7,6},{8,7},{9,8},{10,9},{11,1... | collective-permute-start | bytes 196616 | tf_op jit(solution)/shard_map/ppermute | solution.py:19
  26.4 3.7 %collective-permute-start = (f32[4,4096]{1,0:T(4,128)S(1)}, f32[4,4096]{1,0:T(4,128)S(1)}, u32[]{:S(2)}, u32[]{:S(2)}) collective-permute-start(f32[4,4096]{1,0:T(4,128)S(1)} %get-tuple-element.37), channel_id=1, source_target_pairs={{0,1},{1,2},{2,3},{3,4},{4,5},{5,6},{6,7},{7,8},{8,9},{9,10},{10,1... | collective-permute-start | bytes 196616 | tf_op jit(solution)/shard_map/ppermute | solution.py:19
  30.1 0.1 pad_subtract_fusion.1
  30.2 0.8 collective-permute-done
  31.0 0.1 broadcast_multiply_fusion.1
  31.2 0.1 copy-done.1
  31.2 0.3 add_multiply_fusion.6
  31.6 0.1 slice.290
  31.7 0.3 slice.292
  32.0 0.6 add_multiply_fusion.5
  32.6 0.9 add_multiply_fusion.4
  33.5 0.1 slice.294
  33.6 0.3 slice.296
  33.9 0.4 add_multiply_fusion.3
  34.4 1.0 add_multiply_fusion.2
  35.3 0.1 slice.298
  35.4 0.3 slice.300
  35.8 0.4 add_multiply_fusion.1
  36.2 1.1 add_multiply_fusion
  37.3 0.8 fusion.23
  38.1 0.1 fusion.19
  38.2 0.1 fusion.21
  38.3 0.4 multiply_reduce_fusion.5
  38.7 0.1 fusion.31
  38.8 0.5 add.288
  39.3 0.2 reduce_sum.259
  39.5 0.1 fusion.27
  39.6 0.5 add.283
  40.2 0.2 reduce_sum.253
  40.4 1.0 copy.8
  41.5 78.8 %reduce-scatter.4.cloned.1.call-done = f32[128,2]{1,0:T(8,128)} async-done(((f32[1024,2]{1,0:T(8,128)}), f32[128,2]{1,0:T(8,128)}) %reduce-scatter.4.cloned.1.call-update) | async-done | bytes 1040
  120.2 1.5 %copy.9 = f32[2,128]{1,0:T(2,128)} copy(f32[2,128]{0,1:T(8,128)} %bitcast.46) | data formatting | bytes 2048
  (22 shorter events, 0.1 us)
Async XLA Ops:
  8.4 15.4 %all-to-all-start = ((f32[8,2,128]{2,1,0:T(2,128)}), f32[8,2,128]{2,1,0:T(2,128)S(1)}, u32[]{:S(2)}, u32[]{:S(2)}) async-start(f32[8,2,128]{2,1,0:T(2,128)} %stack.14), calls=%async_computation | async-start | bytes 16384 | tf_op jit(solution)/shard_map/all_to_all | solution.py:65
  16.1 104.1 %reduce-scatter.4.cloned.1.call-start = ((), (), s32[]{:S(2)}) async-start(), calls=%async_computation.2 | async-start | bytes 589824
  16.2 6.6 %copy-start.2 = (s32[4,8,4096]{2,1,0:T(8,128)S(1)}, s32[4,8,4096]{2,1,0:T(8,128)}, u32[]{:S(2)}) copy-start(s32[4,8,4096]{2,1,0:T(8,128)} %param.7) | copy-start | bytes 1572868
  16.2 6.6 %copy-start.3 = (bf16[4,8,4096]{2,1,0:T(8,128)(2,1)S(1)}, bf16[4,8,4096]{2,1,0:T(8,128)(2,1)}, u32[]{:S(2)}) copy-start(bf16[4,8,4096]{2,1,0:T(8,128)(2,1)} %param.8) | copy-start | bytes 786436
  17.6 13.6 %collective-permute-start.3 = (f32[2,2,4,4096]{3,2,1,0:T(4,128)S(1)}, f32[2,2,4,4096]{3,2,1,0:T(4,128)S(1)}, u32[]{:S(2)}, u32[]{:S(2)}) collective-permute-start(f32[2,2,4,4096]{3,2,1,0:T(4,128)S(1)} %get-tuple-element.33), channel_id=1, source_target_pairs={{1,0},{2,1},{3,2},{4,3},{5,4},{6,5},{7,6},{8,7},{9,8},{10,9},{11,1... | collective-permute-start | bytes 786440 | tf_op jit(solution)/shard_map/ppermute | solution.py:19
  18.9 12.3 %collective-permute-start.2 = (f32[2,2,4,4096]{3,2,1,0:T(4,128)S(1)}, f32[2,2,4,4096]{3,2,1,0:T(4,128)S(1)}, u32[]{:S(2)}, u32[]{:S(2)}) collective-permute-start(f32[2,2,4,4096]{3,2,1,0:T(4,128)S(1)} %get-tuple-element.32), channel_id=1, source_target_pairs={{0,1},{1,2},{2,3},{3,4},{4,5},{5,6},{6,7},{7,8},{8,9},{9,10},{10,1... | collective-permute-start | bytes 786440 | tf_op jit(solution)/shard_map/ppermute | solution.py:19
  21.9 0.7 copy-start.4
  25.1 5.1 %collective-permute-start.1 = (f32[4,4096]{1,0:T(4,128)S(1)}, f32[4,4096]{1,0:T(4,128)S(1)}, u32[]{:S(2)}, u32[]{:S(2)}) collective-permute-start(f32[4,4096]{1,0:T(4,128)S(1)} %get-tuple-element.38), channel_id=1, source_target_pairs={{1,0},{2,1},{3,2},{4,3},{5,4},{6,5},{7,6},{8,7},{9,8},{10,9},{11,1... | collective-permute-start | bytes 196616 | tf_op jit(solution)/shard_map/ppermute | solution.py:19
  26.4 4.6 %collective-permute-start = (f32[4,4096]{1,0:T(4,128)S(1)}, f32[4,4096]{1,0:T(4,128)S(1)}, u32[]{:S(2)}, u32[]{:S(2)}) collective-permute-start(f32[4,4096]{1,0:T(4,128)S(1)} %get-tuple-element.37), channel_id=1, source_target_pairs={{0,1},{1,2},{2,3},{3,4},{4,5},{5,6},{6,7},{7,8},{8,9},{9,10},{10,1... | collective-permute-start | bytes 196616 | tf_op jit(solution)/shard_map/ppermute | solution.py:19
  30.2 1.0 copy-start
  30.2 1.0 copy-start.1
Sparse Core Ops, SparseCore 0:
  41.6 78.5 reduce-scatter.3
